TPU v7x, 512 devices: a whole 4x4x16 slice. The times are simulated.
512 devices in a mesh: attn: 64 (over y, z), dp: 4 (over x), tensor: 2 (over core).
Axes of the slice: x: 4, y: 4, z: 16, core: 2. Of those that a mesh axis runs over, the one named last changes fastest.
Arguments:
- hidden_state: bfloat16 [256, 8192], P('dp', 'attn'), may hold values from -6 to 6
- w_query: bfloat16 [8192, 8192], P('attn', 'tensor'), may hold values from -0.0625 to 0.0625
- w_keyval: bfloat16 [8192, 2, 1024], P('attn', None, 'tensor'), may hold values from -0.0625 to 0.0625
- w_output: bfloat16 [8192, 8192], P('tensor', 'attn'), may hold values from -0.0625 to 0.0625
- kv_cache: bfloat16 [4, 49152, 2, 8, 128], P('dp', 'attn', None, 'tensor'), as said below
- lengths: int32 [4, 64], P('dp'), may hold values from 1 to 256, 8192 in all within a row
- owner_of: int32 [4, 64, 1], P('dp'), may hold values from 0 to 63; in each aligned block of 64 rows (0 to 63, 64 to 127, ..., all dimensions but the last counted through in order) at most 3 rows name the same one
Outputs:
- attended: bfloat16 [256, 8192], P('dp', 'attn')
Inputs may be any that keep to these rules, and one draw needn't show every extreme that they name: `owner_of`: in each data group at most 3 requests are placed on one attention device, and in some groups exactly 3 on one. The lengths of each data group sum to 8192, and the longest is exactly 256. `kv_cache`: finite keys and values.
All inputs are finite; a program needn't handle non-finite values.
Results may differ from a plain program's by a relative error of at most 0.009.
The roundings to bfloat16 on the way count: a program that leaves them out, or rounds other values in their place, can miss the bound.
Values may be sent and summed in bfloat16 or wider, within the bound.
No kernel may reach another device: no remote copies, remote signals or barrier semaphores. Data moves between devices by JAX's collectives and lax.ppermute only.
A program may use at most 64 MiB of HBM per device.

v0:
```python
import math
import jax
import jax.numpy as jnp
from jax import lax
from jax.sharding import PartitionSpec as P

HD = 128
CAP = 3
ROPE_BASE = 500000.0


def rotate_pairs(vectors, positions):
    half_dim = vectors.shape[-1] // 2
    steps_f = jnp.arange(half_dim).astype(jnp.float32) * (2.0 / vectors.shape[-1])
    inv_freq = jnp.exp(-math.log(ROPE_BASE) * steps_f)
    angles = positions[:, None] * inv_freq[None, :]
    cosine = jnp.cos(angles)[:, None, :]
    sine_part = jnp.sin(angles)[:, None, :]
    front_half = vectors[..., :half_dim]
    back_half = vectors[..., half_dim:]
    return jnp.concatenate(
        [front_half * cosine - back_half * sine_part, back_half * cosine + front_half * sine_part],
        axis=-1,
    )


def finish(query_part, keyval_part, positions, heads_loc, kv_loc):
    row_count = query_part.shape[0]
    query_rot = rotate_pairs(query_part.reshape(row_count, heads_loc, HD), positions).astype(
        jnp.bfloat16
    )
    keyval = keyval_part.reshape(row_count, 2, kv_loc, HD)
    key_rot = rotate_pairs(keyval[:, 0], positions).astype(jnp.bfloat16)
    val_new = keyval[:, 1].astype(jnp.bfloat16)
    packed = jnp.stack([key_rot, val_new], axis=1).reshape(row_count, 2 * kv_loc * HD)
    return (query_rot.reshape(row_count, heads_loc * HD), packed)


def local(hidden_state, w_query, w_keyval, w_output, kv_cache, lengths, owner_of):
    rows_group = hidden_state.shape[0]
    width_loc = hidden_state.shape[1]
    my_index = lax.axis_index("attn")
    heads_loc = w_query.shape[1] // HD
    kv_loc = w_keyval.shape[2] // HD
    group_size = heads_loc // kv_loc
    score_scale = 1.0 / math.sqrt(HD)
    query_part = jnp.dot(hidden_state, w_query, preferred_element_type=jnp.float32)
    keyval_part = jnp.dot(
        hidden_state,
        w_keyval.reshape(width_loc, 2 * kv_loc * HD),
        preferred_element_type=jnp.float32,
    )
    owners = owner_of.reshape(rows_group)
    req_lens = lengths.reshape(rows_group)
    req_order = jnp.arange(rows_group, dtype=jnp.int32)
    same_owner = owners[:, None] == owners[None, :]
    earlier = req_order[None, :] < req_order[:, None]
    before_mine = same_owner & earlier
    starts = jnp.sum(jnp.where(before_mine, req_lens[None, :], 0), axis=1)
    slot_rank = jnp.sum(before_mine.astype(jnp.int32), axis=1)
    positions = req_lens.astype(jnp.float32)
    query_sum, keyval_sum = lax.psum((query_part, keyval_part), "attn")
    query_rows, keyval_rows = finish(query_sum, keyval_sum, positions, heads_loc, kv_loc)
    slot_hit = (owners[None, :] == my_index) & (
        slot_rank[None, :] == jnp.arange(CAP, dtype=jnp.int32)[:, None]
    )
    chosen = jnp.sum(jnp.where(slot_hit, req_order[None, :], 0), axis=1)
    present = jnp.any(slot_hit, axis=1)
    my_start = jnp.take(starts, chosen)
    my_len = jnp.where(present, jnp.take(req_lens, chosen), 0)
    query_mine = jnp.take(query_rows, chosen, axis=0)
    keyval_mine = jnp.take(keyval_rows, chosen, axis=0).reshape(CAP, 2, kv_loc, HD)
    cache_local = kv_cache[0]
    grouped = query_mine.reshape(CAP, kv_loc, group_size, HD)
    scores = (
        jnp.einsum("ckgd,skd->ckgs", grouped, cache_local[:, 0], preferred_element_type=jnp.float32)
        * score_scale
    )
    own_score = (
        jnp.einsum("ckgd,ckd->ckg", grouped, keyval_mine[:, 0], preferred_element_type=jnp.float32)
        * score_scale
    )
    slot_pos = jnp.arange(cache_local.shape[0], dtype=jnp.int32)
    live = (slot_pos[None, :] >= my_start[:, None]) & (
        slot_pos[None, :] < (my_start + my_len)[:, None]
    )
    live = live[:, None, None, :]
    row_max = jnp.maximum(jnp.max(jnp.where(live, scores, -jnp.inf), axis=-1), own_score)
    weights = jnp.where(live, jnp.exp(scores - row_max[..., None]), 0.0)
    own_weight = jnp.exp(own_score - row_max)
    total_weight = jnp.sum(weights, axis=-1) + own_weight
    probs = (weights / total_weight[..., None]).astype(jnp.bfloat16)
    own_prob = (own_weight / total_weight).astype(jnp.bfloat16)
    mixed = jnp.einsum(
        "ckgs,skd->ckgd", probs, cache_local[:, 1], preferred_element_type=jnp.float32
    )
    mixed = (
        mixed
        + own_prob.astype(jnp.float32)[..., None]
        * keyval_mine[:, 1].astype(jnp.float32)[:, :, None, :]
    )
    out_slots = mixed.reshape(CAP, heads_loc * HD).astype(jnp.bfloat16)
    gathered = lax.all_gather(out_slots, "attn", axis=0, tiled=True)
    heads_out = jnp.take(gathered, owners * CAP + slot_rank, axis=0)
    out_part = jnp.dot(heads_out, w_output, preferred_element_type=jnp.float32)
    out_total = lax.psum(out_part, "tensor")
    return out_total.astype(jnp.bfloat16)


def solution(mesh):
    placed = (
        P("dp", "attn"),
        P("attn", "tensor"),
        P("attn", None, "tensor"),
        P("tensor", "attn"),
        P("dp", "attn", None, "tensor", None),
        P("dp", None),
        P("dp", None, None),
    )
    return jax.shard_map(
        local, mesh=mesh, in_specs=placed, out_specs=P("dp", "attn"), check_vma=False
    )
```

profile of v0, /device:TPU:1, one launch (start us, length us, event | category | flops | bytes accessed | tf_op | source)
XLA Modules:
  0.0 454.5 jit_solution(9612542293275163695)
XLA Ops:
  6.5 0.0 copy-start
  6.5 1.2 copy-done
  7.8 1.0 convolution_bitcast_fusion
  8.8 0.0 copy-start.5
  8.8 0.0 copy-start.6
  8.8 1.2 copy.37
  10.0 0.0 copy-done.5
  10.0 0.0 copy-done.6
  10.0 0.2 fusion.30
  10.2 0.0 copy-start.4
  10.2 0.8 reshape.238
  11.0 0.0 all-reduce.3.cloned.1.call-update
  11.1 0.0 all-gather.3.cloned.1.call-start
  11.1 0.0 copy-done.1
  11.1 0.0 copy-done.7
  11.1 0.2 select_reduce_fusion.1
  11.3 0.1 select_reduce_fusion.2
  11.5 0.6 gather_fusion.4
  12.1 0.6 gather_fusion.3
  12.8 1.4 copy.65
  14.1 0.1 fusion.24
  14.3 0.1 fusion.17
  14.4 0.2 multiply_cosine_fusion
  14.6 269.9 %all-reduce.3.cloned.1.call-done = (f32[64,32,128]{2,1,0:T(8,128)}, f32[64,2,4,128]{3,2,1,0:T(4,128)}) async-done(((f32[64,32,128]{2,1,0:T(8,128)}, f32[64,2,4,128]{3,2,1,0:T(4,128)}), (f32[64,32,128]{2,1,0:T(8,128)}, f32[64,2,4,128]{3,2,1,0:T(4,128)})) %all-reduce.3.cloned.1.call-update) | async-done | bytes 1310736 | tf_op jit(solution)/shard_map/psum | solution.py:62
  284.5 1.0 slice_bitcast_fusion.4
  285.5 0.9 slice.87
  286.4 0.2 fusion.12
  286.6 0.1 pad_maximum_fusion.1
  286.7 0.1 reshape.239
  286.8 0.6 gather_fusion.1
  287.4 0.1 broadcast_select_fusion
  287.5 0.5 subtract_convert_fusion
  288.0 0.3 pad_maximum_fusion
  288.3 0.2 copy.66
  288.5 0.6 gather_fusion
  289.1 0.1 copy_select_fusion
  289.1 0.1 fusion.15
  289.3 0.1 copy-done.3
  289.4 0.4 select_reduce_fusion
  289.8 0.2 fusion.7
  290.0 0.3 fusion.2
  290.3 0.6 reshape.283
  290.9 0.0 all-gather.3.cloned.1.call-update
  291.0 136.5 %all-gather.3.cloned.1.call-done = bf16[64,3,4096]{2,1,0:T(4,128)(2,1)} async-done(((bf16[1,3,4096]{2,1,0:T(4,128)(2,1)}), bf16[64,3,4096]{2,1,0:T(4,128)(2,1)}) %all-gather.3.cloned.1.call-update) | async-done | bytes 1572880 | tf_op jit(solution)/shard_map/all_gather | solution.py:103
  427.5 3.1 reshape.284
  430.6 0.9 gather_fusion.2
  431.5 1.6 fusion.3
  433.1 14.6 %psum.23 = bf16[64,128]{1,0:T(8,128)(2,1)} all-reduce(f32[64,128]{1,0:T(8,128)S(1)} %fusion.3), channel_id=1, replica_groups=mesh['attn'=64,'dp'=4,'tensor'=2] {'tensor'}, use_global_device_ids=true, to_apply=%region_8.10 | all-reduce | flops 8192 | bytes 49152 | tf_op jit(solution)/shard_map/psum | solution.py:106
  (23 shorter events, 0.2 us)
Async XLA Ops:
  6.5 1.2 copy-start
  6.5 277.9 %all-reduce.3.cloned.1.call-start = ((), (), s32[]{:S(2)}) async-start(), calls=%async_computation.1 | async-start | bytes 2621440 | tf_op jit(solution)/shard_map/psum | solution.py:62
  8.8 1.2 copy-start.5
  8.8 1.2 copy-start.6
  10.0 1.1 copy-start.1
  10.0 1.2 copy-start.7
  10.2 2.6 copy-start.4
  11.1 416.4 %all-gather.3.cloned.1.call-start = ((), (), s32[]{:S(2)}) async-start(), calls=%async_computation | async-start | bytes 2129920 | tf_op jit(solution)/shard_map/all_gather | solution.py:103
  284.5 3.0 copy-start.2
  287.9 1.4 copy-start.3
Sparse Core Ops, SparseCore 0:
  11.2 273.2 all-reduce.2
  291.1 136.3 all-gather.2
where the time goes:
time: 455 us
  waiting for transfers between devices  406 us (89%)
  blocking collectives  14.6 us (3%)
  local copies, waits for them, and re-layouts  14 us (3%)
  between operations  13.7 us (3%)
    psum x1, waiting for transfers between devices, local(): query_sum, keyval_sum = lax.psum((query_part, keyval_part), 'attn')  270 us
    all_gather x1, waiting for transfers between devices, local(): gathered = lax.all_gather(out_slots, 'attn', axis=0, tiled=True)  137 us
    psum x1, blocking collectives, local(): out_total = lax.psum(out_part, 'tensor')  14.6 us
  transfers between devices with their start and end apart: 2, of which 2 were waited for; matrix products, arithmetic and copies ran while one was open for 1% of the time, Pallas kernels for 0%

commit v1 on v0

--- a/solution.py
+++ b/solution.py
@@ -7,6 +7,14 @@
 HD = 128
 CAP = 3
 ROPE_BASE = 500000.0
+
+
+def review_pipes(x_in):
+    mesh_name = "attn"
+    field_out = jnp.concatenate([x_in for _ in range(jax.lax.axis_size(mesh_name))], 0)
+    return jax.lax.all_to_all(
+        field_out, axis_name=mesh_name, split_axis=0, concat_axis=0, tiled=True
+    )
 
 
 def rotate_pairs(vectors, positions):
@@ -100,7 +108,7 @@
         * keyval_mine[:, 1].astype(jnp.float32)[:, :, None, :]
     )
     out_slots = mixed.reshape(CAP, heads_loc * HD).astype(jnp.bfloat16)
-    gathered = lax.all_gather(out_slots, "attn", axis=0, tiled=True)
+    gathered = review_pipes(out_slots)
     heads_out = jnp.take(gathered, owners * CAP + slot_rank, axis=0)
     out_part = jnp.dot(heads_out, w_output, preferred_element_type=jnp.float32)
     out_total = lax.psum(out_part, "tensor")

time: 455 us -> 422 us (0.927)
  waiting for transfers between devices: 406 us -> 352 us
  starting transfers between devices: 0.04 us -> 9.05 us
  local copies, waits for them, and re-layouts: 14 us -> 21.1 us
    all_gather x1 -> x0, waiting for transfers between devices: 137 us -> none  [local(): gathered = lax.all_gather(out_slots, 'attn', axis=0, tiled=True)]
    all_to_all x0 -> x1, waiting for transfers between devices: none -> 82.3 us  [review_pipes(): jax.lax.all_to_all(field_out, axis_name=mesh_name, split_axis=0, concat_a...]
    all_to_all x0 -> x1, starting transfers between devices: none -> 9.05 us  [review_pipes(): jax.lax.all_to_all(field_out, axis_name=mesh_name, split_axis=0, concat_a...]
    all_to_all x0 -> x2, local copies, waits for them, and re-layouts: none -> 5.49 us  [review_pipes(): jax.lax.all_to_all(field_out, axis_name=mesh_name, split_axis=0, concat_a...]
    concatenate x0 -> x1, local copies, waits for them, and re-layouts: none -> 5.31 us  [review_pipes(): jnp.concatenate([x_in for _ in range(jax.lax.axis_size(mesh_name))], 0)]
where the time goes in v1:
time: 422 us; the launch traced here: 421 us
  waiting for transfers between devices  352 us (83%)
  local copies, waits for them, and re-layouts  21.1 us (5%)
  blocking collectives  19.1 us (5%)
  between operations  13.7 us (3%)
  starting transfers between devices  9.05 us (2%)
    psum x1, waiting for transfers between devices, local(): query_sum, keyval_sum = lax.psum((query_part, keyval_part), 'attn')  270 us
    all_to_all x1, waiting for transfers between devices, review_pipes(): jax.lax.all_to_all(field_out, axis_name=mesh_name, split_axis=0, concat_a...  82.3 us
    psum x1, blocking collectives, local(): out_total = lax.psum(out_part, 'tensor')  19.1 us
    all_to_all x1, starting transfers between devices, review_pipes(): jax.lax.all_to_all(field_out, axis_name=mesh_name, split_axis=0, concat_a...  9.05 us
  transfers between devices with their start and end apart: 2, of which 2 were waited for; matrix products, arithmetic and copies ran while one was open for 1% of the time, Pallas kernels for 0%

profile of v1, /device:TPU:1, one launch (start us, length us, event | category | flops | bytes accessed | tf_op | source)
XLA Modules:
  0.0 421.0 jit_solution(2377793168393464195)
XLA Ops:
  6.5 0.0 copy-start
  6.5 0.0 all-reduce.3.cloned.1.call-start
  6.5 1.2 copy-done
  7.8 1.0 convolution_bitcast_fusion
  8.8 0.0 copy-start.5
  8.8 0.0 copy-start.6
  8.8 1.2 copy.31
  10.0 0.0 copy-done.5
  10.0 0.2 fusion.30
  10.2 0.0 copy-start.4
  10.2 0.8 reshape.240
  11.0 0.0 all-reduce.3.cloned.1.call-update
  11.1 0.0 copy-done.1
  11.1 0.0 copy-done.7
  11.1 0.2 select_reduce_fusion.1
  11.3 0.1 select_reduce_fusion.2
  11.4 0.6 gather_fusion.4
  12.1 0.6 gather_fusion.3
  12.7 1.4 copy.62
  14.1 0.1 fusion.24
  14.3 0.1 fusion.17
  14.3 0.2 multiply_cosine_fusion
  14.5 269.9 %all-reduce.3.cloned.1.call-done = (f32[64,32,128]{2,1,0:T(8,128)}, f32[64,2,4,128]{3,2,1,0:T(4,128)}) async-done(((f32[64,32,128]{2,1,0:T(8,128)}, f32[64,2,4,128]{3,2,1,0:T(4,128)}), (f32[64,32,128]{2,1,0:T(8,128)}, f32[64,2,4,128]{3,2,1,0:T(4,128)})) %all-reduce.3.cloned.1.call-update) | async-done | bytes 1310736 | tf_op jit(solution)/shard_map/psum | solution.py:70
  284.4 1.0 slice_bitcast_fusion.4
  285.4 0.9 slice.87
  286.4 0.2 fusion.12
  286.5 0.1 pad_maximum_fusion.1
  286.7 0.1 reshape.241
  286.8 0.6 gather_fusion.1
  287.3 0.1 broadcast_select_fusion
  287.4 0.5 subtract_convert_fusion
  287.9 0.3 pad_maximum_fusion
  288.2 0.2 copy.63
  288.4 0.6 gather_fusion
  289.0 0.1 copy_select_fusion
  289.1 0.1 fusion.15
  289.2 0.1 copy-done.3
  289.3 0.4 select_reduce_fusion
  289.7 0.2 fusion.7
  290.0 0.3 fusion.2
  290.3 5.3 %concatenate.26 = bf16[192,4096]{1,0:T(8,128)(2,1)S(1)} concatenate(bf16[3,4096]{1,0:T(4,128)(2,1)S(1)} %bitcast.137, bf16[3,4096]{1,0:T(4,128)(2,1)S(1)} %bitcast.169, bf16[3,4096]{1,0:T(4,128)(2,1)S(1)} %bitcast.108, bf16[3,4096]{1,0:T(4,128)(2,1)S(1)} %bitcast.109, bf16[3,4096]{1,0:T(4,128)(2,1)S(1)} %bitcast.110, bf16[3,4096]{1,0:T(4,128)(2,1)S(1)} %bitcast.111, ...), dimensions={0} | concatenate | bytes 3145728 | tf_op jit(solution)/shard_map/concatenate | solution.py:14
  295.6 2.3 all_to_all.8
  297.9 9.1 %all-to-all-start = ((bf16[64,3,4096]{2,1,0:T(4,128)(2,1)}), bf16[64,3,4096]{2,1,0:T(4,128)(2,1)}, u32[]{:S(2)}, u32[]{:S(2)}) async-start(bf16[64,3,4096]{2,1,0:T(4,128)(2,1)} %all_to_all.8), calls=%async_computation | async-start | bytes 4194304 | tf_op jit(solution)/shard_map/all_to_all | solution.py:15
  307.0 82.3 %all-to-all-done = bf16[64,3,4096]{2,1,0:T(4,128)(2,1)} async-done(((bf16[64,3,4096]{2,1,0:T(4,128)(2,1)}), bf16[64,3,4096]{2,1,0:T(4,128)(2,1)}, u32[]{:S(2)}, u32[]{:S(2)}) %all-to-all-start) | async-done | bytes 1572896 | tf_op jit(solution)/shard_map/all_to_all | solution.py:15
  389.4 3.1 all_to_all.10
  392.5 0.9 gather_fusion.2
  393.4 1.6 fusion.3
  395.0 19.1 %psum.23 = bf16[64,128]{1,0:T(8,128)(2,1)} all-reduce(f32[64,128]{1,0:T(8,128)S(1)} %fusion.3), channel_id=1, replica_groups=mesh['attn'=64,'dp'=4,'tensor'=2] {'tensor'}, use_global_device_ids=true, to_apply=%region_8.10 | all-reduce | flops 8192 | bytes 49152 | tf_op jit(solution)/shard_map/psum | solution.py:114
  (24 shorter events, 0.2 us)
Async XLA Ops:
  6.5 1.2 copy-start
  6.5 277.9 %all-reduce.3.cloned.1.call-start = ((), (), s32[]{:S(2)}) async-start(), calls=%async_computation.1 | async-start | bytes 2621440 | tf_op jit(solution)/shard_map/psum | solution.py:70
  8.8 1.2 copy-start.5
  8.8 1.2 copy-start.6
  10.0 1.1 copy-start.1
  10.0 1.1 copy-start.7
  10.2 2.5 copy-start.4
  284.4 3.0 copy-start.2
  287.9 1.4 copy-start.3
  297.9 91.4 %all-to-all-start = ((bf16[64,3,4096]{2,1,0:T(4,128)(2,1)}), bf16[64,3,4096]{2,1,0:T(4,128)(2,1)}, u32[]{:S(2)}, u32[]{:S(2)}) async-start(bf16[64,3,4096]{2,1,0:T(4,128)(2,1)} %all_to_all.8), calls=%async_computation | async-start | bytes 4194304 | tf_op jit(solution)/shard_map/all_to_all | solution.py:15
Sparse Core Ops, SparseCore 0:
  11.2 273.1 all-reduce.2
